TPU v7x, 32 devices: a whole 2x2x4 slice. The times are simulated.
32 devices in a mesh: rep: 8 (over z, core), tp: 4 (over y, x).
Axes of the slice: x: 2, y: 2, z: 4, core: 2. Of those that a mesh axis runs over, the one named last changes fastest.
Arguments:
- partials: bfloat16 [512, 32768], P('rep', 'tp'), may hold values from -6 to 6
- residual: bfloat16 [512, 8192], P('rep', 'tp'), may hold values from -6 to 6
- lower: bfloat16 [512, 8192], P('rep', 'tp'), may hold values from -6 to 6
- middle: bfloat16 [512, 8192], P('rep', 'tp'), may hold values from -6 to 6
- accepted: int32 [256], P('rep'), may hold values from 0 to 63
- fc_weight: bfloat16 [3, 8192, 8192], P(None, 'rep', 'tp')
- norm_gain: float32 [8192], P('tp'), may hold values from 0.1 to 1.9
- grad_normed: bfloat16 [256, 8192], P('rep', 'tp')
Outputs:
- normed: bfloat16 [256, 8192], P('rep', 'tp')
- grad_fc: bfloat16 [3, 8192, 8192], P(None, 'rep', 'tp')
All inputs are finite; a program needn't handle non-finite values.
Results may differ from a plain program's by a relative error of at most 0.017.
Values may be sent and summed in bfloat16 or wider, within the bound.
No kernel may reach another device: no remote copies, remote signals or barrier semaphores. Data moves between devices by JAX's collectives and lax.ppermute only.
A program may use at most 64 MiB of HBM per device.

v0:
```python
import jax
import jax.numpy as jnp
from jax import lax
from jax.sharding import PartitionSpec as P

D = 8192
EPSILON = 1e-06


def xor_exchange(chunk_of, axis, size):
    for k in range(1, size):
        perm = [(i, i ^ k) for i in range(size)]
        yield lax.ppermute(chunk_of(k), axis, perm)


def body(partials, residual, lower, middle, accepted, fc_weight, norm_gain, grad_normed):
    rep_count = lax.axis_size("rep")
    tp_count = lax.axis_size("tp")
    rep_index = lax.axis_index("rep")
    tp_index = lax.axis_index("tp")
    rows = accepted.shape[0]
    tp_width = residual.shape[1]
    picked = jnp.take(partials, accepted, axis=0).reshape(rows, tp_count, tp_width)
    summed = jnp.take(picked, tp_index, axis=1).astype(jnp.float32)
    for got in xor_exchange(lambda k: jnp.take(picked, tp_index ^ k, axis=1), "tp", tp_count):
        summed = summed + got.astype(jnp.float32)
    upper_rows = (jnp.take(residual, accepted, axis=0).astype(jnp.float32) + summed).astype(
        jnp.bfloat16
    )
    local_rows = jnp.stack(
        [jnp.take(lower, accepted, axis=0), jnp.take(middle, accepted, axis=0), upper_rows], axis=1
    )
    slab_width = D // rep_count
    group = rep_count // tp_count
    slabs = local_rows.reshape(rows, 3, group, slab_width)
    received = []
    for c in range(group):
        perm = []
        for r in range(rep_count):
            for t in range(tp_count):
                s = group * t + (r - c) % group
                perm.append((r * tp_count + t, s * tp_count + r // group))
        block = jnp.take(slabs, (rep_index - c) % group, axis=2)
        received.append(lax.ppermute(block, ("rep", "tp"), perm))
    stacked = jnp.stack(received, axis=0)
    order = (jnp.arange(group, dtype=jnp.int32) - rep_index) % group
    mine = jnp.take(stacked, order, axis=0).reshape(group * rows, 3, slab_width)
    features = lax.all_gather(mine, "tp", axis=0, tiled=True)
    total_rows = features.shape[0]
    feature_flat = features.reshape(total_rows, 3 * slab_width)
    fc_block = fc_weight.reshape(3 * slab_width, fc_weight.shape[2])
    hidden = lax.psum_scatter(
        jnp.dot(feature_flat, fc_block, preferred_element_type=jnp.float32),
        "rep",
        scatter_dimension=0,
        tiled=True,
    )
    squares = lax.psum(jnp.sum(hidden * hidden, axis=1), "tp")
    inv_rms = lax.rsqrt(squares / D + EPSILON)
    normed = (hidden * inv_rms[:, None] * norm_gain).astype(jnp.bfloat16)
    scaled = grad_normed.astype(jnp.float32) * norm_gain
    inner_sum = lax.psum(jnp.sum(scaled * hidden, axis=1), "tp")
    hidden_grads = (
        inv_rms[:, None] * scaled - hidden * (inv_rms**3 * inner_sum / D)[:, None]
    ).astype(jnp.bfloat16)
    hidden_grads_all = lax.all_gather(hidden_grads, "rep", axis=0, tiled=True)
    grad_fc = lax.dot_general(
        feature_flat, hidden_grads_all, (((0,), (0,)), ((), ())), preferred_element_type=jnp.float32
    )
    grad_fc = grad_fc.reshape(fc_weight.shape).astype(jnp.bfloat16)
    return (normed, grad_fc)


def solution(mesh):
    in_specs = (
        P("rep", "tp"),
        P("rep", "tp"),
        P("rep", "tp"),
        P("rep", "tp"),
        P("rep"),
        P(None, "rep", "tp"),
        P("tp"),
        P("rep", "tp"),
    )
    out_specs = (P("rep", "tp"), P(None, "rep", "tp"))
    return jax.shard_map(body, mesh=mesh, in_specs=in_specs, out_specs=out_specs, check_vma=False)
```

profile of v0, /device:TPU:0, one launch (start us, length us, event | category | flops | bytes accessed | tf_op | source)
XLA Modules:
  0.0 174.8 jit_solution(10353855674359227189)
XLA Ops:
  7.2 0.0 copy-start
  7.2 0.0 all-gather.3.cloned.1.call-start
  7.3 0.7 compare_and_fusion
  8.0 0.7 compare_select_fusion
  8.7 0.0 copy-done
  8.7 0.9 gather_fusion
  9.5 0.0 copy-start.1
  9.6 0.0 copy-start.2
  9.6 0.0 copy-start.3
  9.6 0.1 bitcast_select_fusion
  9.8 3.0 %collective-permute-start = (bf16[32,2048]{1,0:T(8,128)(2,1)S(1)}, bf16[32,2048]{1,0:T(8,128)(2,1)S(1)}, u32[]{:S(2)}, u32[]{:S(2)}) collective-permute-start(bf16[32,2048]{1,0:T(8,128)(2,1)S(1)} %get-tuple-element.31), channel_id=1, source_target_pairs={{0,1},{1,0},{2,3},{3,2},{4,5},{5,4},{6,7},{7,6},{8,9},{9,8},{10,11... | collective-permute-start | bytes 393224 | tf_op jit(solution)/shard_map/ppermute | solution.py:13
  12.8 1.5 collective-permute-start.2
  14.3 0.1 collective-permute-start.1
  14.3 0.1 broadcast_in_dim.58
  14.4 0.1 broadcast_in_dim.59
  14.5 0.0 copy-done.1
  14.5 0.6 gather_fusion.4
  15.2 0.0 copy-done.2
  15.2 0.7 gather_fusion.3
  15.8 0.0 copy-done.3
  15.8 0.7 gather_fusion.2
  16.5 0.1 broadcast_select_fusion
  16.6 0.1 stack.22
  16.7 0.1 stack.21
  16.8 0.0 collective-permute-done
  16.9 3.6 %collective-permute-done.2 = bf16[32,2048]{1,0:T(8,128)(2,1)S(1)} collective-permute-done((bf16[32,2048]{1,0:T(8,128)(2,1)S(1)}, bf16[32,2048]{1,0:T(8,128)(2,1)S(1)}, u32[]{:S(2)}, u32[]{:S(2)}) %collective-permute-start.2) | collective-permute-done | bytes 131104 | tf_op jit(solution)/shard_map/ppermute | solution.py:13
  20.4 1.4 collective-permute-done.1
  21.8 0.1 add_convert_fusion
  21.9 0.1 stack.23
  22.1 0.7 collective-permute-start.3
  22.7 0.1 collective-permute-start.4
  22.8 0.0 collective-permute-done.3
  22.9 1.4 collective-permute-done.4
  24.3 0.6 gather_fusion.1
  24.9 0.9 bitcast_select_fusion.1
  25.8 0.0 all-gather.3.cloned.1.call-update
  25.8 0.0 reduce-scatter.2.cloned.1.call-start
  25.8 57.1 %all-gather.3.cloned.1.call-done = bf16[256,3,1024]{2,0,1:T(8,128)(2,1)} async-done(((bf16[64,3,1024]{2,0,1:T(8,128)(2,1)}), bf16[256,3,1024]{2,0,1:T(8,128)(2,1)}) %all-gather.3.cloned.1.call-update) | async-done | bytes 1572880 | tf_op jit(solution)/shard_map/all_gather | solution.py:48
  82.9 9.8 %convolution_bitcast_fusion = f32[256,2048]{1,0:T(8,128)} fusion(bf16[256,3,1024]{2,0,1:T(8,128)(2,1)} %all-gather.3.cloned.1.call-done, bf16[3,1024,2048]{2,1,0:T(8,128)(2,1)} %param.19), kind=kOutput, calls=%fused_computation.6 | convolution fusion | flops 3221225472 | bytes 16252928 | tf_op jit(solution)/shard_map/dot_general | solution.py:53
  92.7 0.0 copy-start.4
  92.7 0.0 copy-start.5
  92.7 0.0 reduce-scatter.2.cloned.1.call-update
  92.8 0.0 all-gather.5.cloned.1.call-start
  92.8 36.2 %reduce-scatter.2.cloned.1.call-done = f32[32,2048]{1,0:T(8,128)} async-done(((f32[256,2048]{1,0:T(8,128)}), f32[32,2048]{1,0:T(8,128)}) %reduce-scatter.2.cloned.1.call-update) | async-done | bytes 262160 | tf_op jit(solution)/shard_map/reduce_scatter | solution.py:52
  129.0 0.0 copy-done.4
  129.0 0.0 copy-done.5
  129.0 1.1 multiply_reduce_fusion
  130.1 9.8 %all-reduce = (f32[32]{0:T(128)S(1)}, f32[32]{0:T(128)S(1)}) all-reduce(f32[32]{0:T(128)S(1)} %get-tuple-element.28, f32[32]{0:T(128)S(1)} %get-tuple-element.27), channel_id=1, replica_groups=mesh['rep'=8,'tp'=4] {'tp'}, use_global_device_ids=true, to_apply=%region_2.6 | all-reduce | flops 64 | bytes 512 | tf_op jit(solution)/shard_map/psum | solution.py:58
  139.9 1.8 %subtract_convert_fusion = (bf16[32,2048]{1,0:T(8,128)(2,1)}, bf16[32,2048]{1,0:T(8,128)(2,1)}) fusion(f32[32,2048]{1,0:T(8,128)} %reduce-scatter.2.cloned.1.call-done, bf16[32,2048]{1,0:T(8,128)(2,1)S(1)} %copy-done.4, f32[32]{0:T(128)S(1)} %get-tuple-element.38, f32[2048]{0:T(1024)S(1)} %copy-done.5, f32[32]{0:T(128)S(1)} %get-tuple-element.39), kind=kLoop, calls=%fused_computation.12 | loop fusion | flops 589824 | bytes 663808 | tf_op jit(solution)/shard_map/convert_element_type | solution.py:65
  141.7 0.0 all-gather.5.cloned.1.call-update
  141.7 1.7 copy.16
  143.4 17.0 %all-gather.5.cloned.1.call-done = bf16[256,2048]{1,0:T(8,128)(2,1)} async-done(((bf16[32,2048]{1,0:T(8,128)(2,1)}), bf16[256,2048]{1,0:T(8,128)(2,1)}) %all-gather.5.cloned.1.call-update) | async-done | bytes 1048592 | tf_op jit(solution)/shard_map/all_gather | solution.py:66
  160.5 7.8 %convolution_convert_fusion = bf16[3,1024,2048]{2,1,0:T(8,128)(2,1)} fusion(bf16[256,3,1024]{0,2,1:T(8,128)(2,1)S(1)} %copy.16, bf16[256,2048]{1,0:T(8,128)(2,1)} %all-gather.5.cloned.1.call-done), kind=kOutput, calls=%fused_computation.5 | convolution fusion | flops 3227516928 | bytes 15204352 | tf_op jit(solution)/shard_map/dot_general | solution.py:67
  (12 shorter events, 0.3 us)
Async XLA Ops:
  7.2 1.5 copy-start
  7.2 75.8 %all-gather.3.cloned.1.call-start = ((), (), s32[]{:S(2)}) async-start(), calls=%async_computation.1 | async-start | bytes 1966080 | tf_op jit(solution)/shard_map/all_gather | solution.py:48
  9.5 5.0 %copy-start.1 = (bf16[64,2048]{1,0:T(8,128)(2,1)S(1)}, bf16[64,2048]{1,0:T(8,128)(2,1)}, u32[]{:S(2)}) copy-start(bf16[64,2048]{1,0:T(8,128)(2,1)} %param.15) | copy-start | bytes 786436
  9.6 5.6 %copy-start.2 = (bf16[64,2048]{1,0:T(8,128)(2,1)S(1)}, bf16[64,2048]{1,0:T(8,128)(2,1)}, u32[]{:S(2)}) copy-start(bf16[64,2048]{1,0:T(8,128)(2,1)} %param.17) | copy-start | bytes 786436
  9.6 6.3 %copy-start.3 = (bf16[64,2048]{1,0:T(8,128)(2,1)S(1)}, bf16[64,2048]{1,0:T(8,128)(2,1)}, u32[]{:S(2)}) copy-start(bf16[64,2048]{1,0:T(8,128)(2,1)} %param.16) | copy-start | bytes 786436
  9.8 7.1 %collective-permute-start = (bf16[32,2048]{1,0:T(8,128)(2,1)S(1)}, bf16[32,2048]{1,0:T(8,128)(2,1)S(1)}, u32[]{:S(2)}, u32[]{:S(2)}) collective-permute-start(bf16[32,2048]{1,0:T(8,128)(2,1)S(1)} %get-tuple-element.31), channel_id=1, source_target_pairs={{0,1},{1,0},{2,3},{3,2},{4,5},{5,4},{6,7},{7,6},{8,9},{9,8},{10,11... | collective-permute-start | bytes 393224 | tf_op jit(solution)/shard_map/ppermute | solution.py:13
  12.8 7.6 %collective-permute-start.2 = (bf16[32,2048]{1,0:T(8,128)(2,1)S(1)}, bf16[32,2048]{1,0:T(8,128)(2,1)S(1)}, u32[]{:S(2)}, u32[]{:S(2)}) collective-permute-start(bf16[32,2048]{1,0:T(8,128)(2,1)S(1)} %get-tuple-element.32), channel_id=1, source_target_pairs={{0,3},{1,2},{2,1},{3,0},{4,7},{5,6},{6,5},{7,4},{8,11},{9,10},{10,... | collective-permute-start | bytes 393224 | tf_op jit(solution)/shard_map/ppermute | solution.py:13
  14.3 7.5 %collective-permute-start.1 = (bf16[32,2048]{1,0:T(8,128)(2,1)S(1)}, bf16[32,2048]{1,0:T(8,128)(2,1)S(1)}, u32[]{:S(2)}, u32[]{:S(2)}) collective-permute-start(bf16[32,2048]{1,0:T(8,128)(2,1)S(1)} %get-tuple-element.33), channel_id=1, source_target_pairs={{0,2},{1,3},{2,0},{3,1},{4,6},{5,7},{6,4},{7,5},{8,10},{9,11},{10,... | collective-permute-start | bytes 393224 | tf_op jit(solution)/shard_map/ppermute | solution.py:13
  22.1 0.8 collective-permute-start.3
  22.7 1.5 collective-permute-start.4
  25.8 103.2 %reduce-scatter.2.cloned.1.call-start = ((), (), s32[]{:S(2)}) async-start(), calls=%async_computation.2 | async-start | bytes 2359296 | tf_op jit(solution)/shard_map/reduce_scatter | solution.py:52
  92.7 36.3 %copy-start.4 = (bf16[32,2048]{1,0:T(8,128)(2,1)S(1)}, bf16[32,2048]{1,0:T(8,128)(2,1)}, u32[]{:S(2)}) copy-start(bf16[32,2048]{1,0:T(8,128)(2,1)} %param.21) | copy-start | bytes 393220
  92.7 36.3 %copy-start.5 = (f32[2048]{0:T(1024)S(1)}, f32[2048]{0:T(1024)}, u32[]{:S(2)}) copy-start(f32[2048]{0:T(1024)} %param.20) | copy-start | bytes 24580
  92.8 67.7 %all-gather.5.cloned.1.call-start = ((), (), s32[]{:S(2)}) async-start(), calls=%async_computation.3 | async-start | bytes 1179648 | tf_op jit(solution)/shard_map/all_gather | solution.py:66
Sparse Core Ops, SparseCore 0:
  25.9 56.9 all-gather.2
  92.9 36.0 reduce-scatter.1
  141.8 18.5 all-gather.4
where the time goes:
time: 175 us
  waiting for transfers between devices  117 us (67%)
  matrix products  17.6 us (10%)
  between operations  14 us (8%)
  blocking collectives  9.79 us (6%)
  local copies, waits for them, and re-layouts  5.65 us (3%)
  other arithmetic  5.65 us (3%)
  starting transfers between devices  5.44 us (3%)
    all_gather x1, waiting for transfers between devices, body(): features = lax.all_gather(mine, 'tp', axis=0, tiled=True)  57.1 us
    reduce_scatter x1, waiting for transfers between devices, body(): lax.psum_scatter(jnp.dot(feature_flat, fc_block, preferred_element_type=j...  36.2 us
    all_gather x1, waiting for transfers between devices, body(): hidden_grads_all = lax.all_gather(hidden_grads, 'rep', axis=0, tiled=True)  17 us
    psum x1, blocking collectives, body(): squares = lax.psum(jnp.sum(hidden * hidden, axis=1), 'tp')  9.79 us
    dot_general x1, matrix products, body(): jnp.dot(feature_flat, fc_block, preferred_element_type=jnp.float32)  9.79 us
    dot_general x1, matrix products, body(): lax.dot_general(feature_flat, hidden_grads_all, (((0,), (0,)), ((), ())),...  7.8 us
    ppermute x3, waiting for transfers between devices, xor_exchange(): yield lax.ppermute(chunk_of(k), axis, perm)  4.92 us
    ppermute x3, starting transfers between devices, xor_exchange(): yield lax.ppermute(chunk_of(k), axis, perm)  4.57 us
  transfers between devices with their start and end apart: 8, of which 6 were waited for; matrix products, arithmetic and copies ran while one was open for 2% of the time, Pallas kernels for 0%

commit v1 on v0

--- a/solution.py
+++ b/solution.py
@@ -5,6 +5,18 @@
 
 D = 8192
 EPSILON = 1e-06
+
+
+def collect(shard, axis, dim):
+    ways, here = (lax.axis_size(axis), lax.axis_index(axis))
+    grown, reach = (shard, 1)
+    while reach < ways:
+        theirs = lax.ppermute(grown, axis, [(d, d ^ reach) for d in range(ways)])
+        mine_first = jnp.concatenate([grown, theirs], axis=dim)
+        theirs_first = jnp.concatenate([theirs, grown], axis=dim)
+        grown = jnp.where(here & reach == 0, mine_first, theirs_first)
+        reach = 2 * reach
+    return grown
 
 
 def xor_exchange(chunk_of, axis, size):
@@ -63,7 +75,7 @@
     hidden_grads = (
         inv_rms[:, None] * scaled - hidden * (inv_rms**3 * inner_sum / D)[:, None]
     ).astype(jnp.bfloat16)
-    hidden_grads_all = lax.all_gather(hidden_grads, "rep", axis=0, tiled=True)
+    hidden_grads_all = collect(hidden_grads, "rep", 0)
     grad_fc = lax.dot_general(
         feature_flat, hidden_grads_all, (((0,), (0,)), ((), ())), preferred_element_type=jnp.float32
     )

time: 175 us -> 192 us (1.097)
  waiting for transfers between devices: 117 us -> 133 us
    ppermute x0 -> x3, waiting for transfers between devices: none -> 33.3 us  [collect(): theirs = lax.ppermute(grown, axis, [(d, d ^ reach) for d in range(ways)])]
    all_gather x1 -> x0, waiting for transfers between devices: 17 us -> none  [body(): hidden_grads_all = lax.all_gather(hidden_grads, 'rep', axis=0, tiled=True)]
  transfers between devices with their start and end apart: 8 -> 10, of which waited for: 6 -> 8; matrix products, arithmetic and copies ran while one was open for 2% -> 2% of each run, Pallas kernels for 0% -> 0%
where the time goes in v1:
time: 192 us
  waiting for transfers between devices  133 us (69%)
  matrix products  17.6 us (9%)
  between operations  14.3 us (7%)
  blocking collectives  9.79 us (5%)
  other arithmetic  5.74 us (3%)
  local copies, waits for them, and re-layouts  5.65 us (3%)
  starting transfers between devices  5.54 us (3%)
    all_gather x1, waiting for transfers between devices, body(): features = lax.all_gather(mine, 'tp', axis=0, tiled=True)  57.1 us
    reduce_scatter x1, waiting for transfers between devices, body(): lax.psum_scatter(jnp.dot(feature_flat, fc_block, preferred_element_type=j...  36.2 us
    ppermute x3, waiting for transfers between devices, collect(): theirs = lax.ppermute(grown, axis, [(d, d ^ reach) for d in range(ways)])  33.3 us
    psum x1, blocking collectives, body(): squares = lax.psum(jnp.sum(hidden * hidden, axis=1), 'tp')  9.79 us
    dot_general x1, matrix products, body(): jnp.dot(feature_flat, fc_block, preferred_element_type=jnp.float32)  9.79 us
    dot_general x1, matrix products, body(): lax.dot_general(feature_flat, hidden_grads_all, (((0,), (0,)), ((), ())),...  7.81 us
    ppermute x3, waiting for transfers between devices, xor_exchange(): yield lax.ppermute(chunk_of(k), axis, perm)  4.92 us
    ppermute x3, starting transfers between devices, xor_exchange(): yield lax.ppermute(chunk_of(k), axis, perm)  4.57 us
  transfers between devices with their start and end apart: 10, of which 8 were waited for; matrix products, arithmetic and copies ran while one was open for 2% of the time, Pallas kernels for 0%

profile of v1, /device:TPU:0, one launch (start us, length us, event | category | flops | bytes accessed | tf_op | source)
XLA Modules:
  0.0 191.6 jit_solution(13175598719970347380)
XLA Ops:
  7.2 0.0 copy-start
  7.2 0.0 all-gather.2.cloned.1.call-start
  7.3 0.7 compare_and_fusion
  8.0 0.7 compare_select_fusion
  8.7 0.0 copy-done
  8.7 0.9 gather_fusion
  9.5 0.0 copy-start.1
  9.6 0.0 copy-start.2
  9.6 0.0 copy-start.3
  9.6 0.1 bitcast_select_fusion
  9.8 3.0 %collective-permute-start = (bf16[32,2048]{1,0:T(8,128)(2,1)S(1)}, bf16[32,2048]{1,0:T(8,128)(2,1)S(1)}, u32[]{:S(2)}, u32[]{:S(2)}) collective-permute-start(bf16[32,2048]{1,0:T(8,128)(2,1)S(1)} %get-tuple-element.31), channel_id=1, source_target_pairs={{0,1},{1,0},{2,3},{3,2},{4,5},{5,4},{6,7},{7,6},{8,9},{9,8},{10,11... | collective-permute-start | bytes 393224 | tf_op jit(solution)/shard_map/ppermute | solution.py:25
  12.8 1.5 collective-permute-start.2
  14.3 0.1 collective-permute-start.1
  14.3 0.1 broadcast_in_dim.58
  14.4 0.1 broadcast_in_dim.59
  14.5 0.0 copy-done.1
  14.5 0.6 gather_fusion.4
  15.2 0.0 copy-done.2
  15.2 0.7 gather_fusion.3
  15.8 0.0 copy-done.3
  15.8 0.7 gather_fusion.2
  16.5 0.1 broadcast_select_fusion
  16.6 0.1 stack.22
  16.7 0.1 stack.21
  16.8 0.0 collective-permute-done
  16.9 3.6 %collective-permute-done.2 = bf16[32,2048]{1,0:T(8,128)(2,1)S(1)} collective-permute-done((bf16[32,2048]{1,0:T(8,128)(2,1)S(1)}, bf16[32,2048]{1,0:T(8,128)(2,1)S(1)}, u32[]{:S(2)}, u32[]{:S(2)}) %collective-permute-start.2) | collective-permute-done | bytes 131104 | tf_op jit(solution)/shard_map/ppermute | solution.py:25
  20.4 1.4 collective-permute-done.1
  21.8 0.1 add_convert_fusion
  21.9 0.1 stack.23
  22.1 0.7 collective-permute-start.3
  22.7 0.1 collective-permute-start.4
  22.8 0.0 collective-permute-done.3
  22.9 1.4 collective-permute-done.4
  24.3 0.6 gather_fusion.1
  24.9 0.9 bitcast_select_fusion.1
  25.8 0.0 all-gather.2.cloned.1.call-update
  25.8 0.0 reduce-scatter.2.cloned.1.call-start
  25.8 57.1 %all-gather.2.cloned.1.call-done = bf16[256,3,1024]{2,0,1:T(8,128)(2,1)} async-done(((bf16[64,3,1024]{2,0,1:T(8,128)(2,1)}), bf16[256,3,1024]{2,0,1:T(8,128)(2,1)}) %all-gather.2.cloned.1.call-update) | async-done | bytes 1572880 | tf_op jit(solution)/shard_map/all_gather | solution.py:60
  82.9 9.8 %convolution_bitcast_fusion = f32[256,2048]{1,0:T(8,128)} fusion(bf16[256,3,1024]{2,0,1:T(8,128)(2,1)} %all-gather.2.cloned.1.call-done, bf16[3,1024,2048]{2,1,0:T(8,128)(2,1)} %param.19), kind=kOutput, calls=%fused_computation.6 | convolution fusion | flops 3221225472 | bytes 16252928 | tf_op jit(solution)/shard_map/dot_general | solution.py:65
  92.7 0.0 copy-start.4
  92.7 0.0 copy-start.5
  92.7 0.0 reduce-scatter.2.cloned.1.call-update
  92.8 36.2 %reduce-scatter.2.cloned.1.call-done = f32[32,2048]{1,0:T(8,128)} async-done(((f32[256,2048]{1,0:T(8,128)}), f32[32,2048]{1,0:T(8,128)}) %reduce-scatter.2.cloned.1.call-update) | async-done | bytes 262160 | tf_op jit(solution)/shard_map/reduce_scatter | solution.py:64
  129.0 0.0 copy-done.4
  129.0 0.0 copy-done.5
  129.0 1.1 multiply_reduce_fusion
  130.1 9.8 %all-reduce = (f32[32]{0:T(128)S(1)}, f32[32]{0:T(128)S(1)}) all-reduce(f32[32]{0:T(128)S(1)} %get-tuple-element.28, f32[32]{0:T(128)S(1)} %get-tuple-element.27), channel_id=1, replica_groups=mesh['rep'=8,'tp'=4] {'tp'}, use_global_device_ids=true, to_apply=%region_2.6 | all-reduce | flops 64 | bytes 512 | tf_op jit(solution)/shard_map/psum | solution.py:70
  139.9 1.7 subtract_convert_fusion
  141.6 0.0 collective-permute-start.5
  141.6 1.3 collective-permute-done.5
  143.0 0.1 collective-permute-start.6
  143.1 8.3 %collective-permute-done.6 = bf16[64,2048]{1,0:T(8,128)(2,1)S(1)} collective-permute-done((bf16[64,2048]{1,0:T(8,128)(2,1)S(1)}, bf16[64,2048]{1,0:T(8,128)(2,1)S(1)}, u32[]{:S(2)}, u32[]{:S(2)}) %collective-permute-start.6) | collective-permute-done | bytes 262176 | tf_op jit(solution)/shard_map/ppermute | solution.py:14
  151.5 0.1 maximum_select_fusion.1
  151.6 0.1 collective-permute-start.7
  151.7 1.7 copy.16
  153.4 23.6 %collective-permute-done.7 = bf16[128,2048]{1,0:T(8,128)(2,1)} collective-permute-done((bf16[128,2048]{1,0:T(8,128)(2,1)S(1)}, bf16[128,2048]{1,0:T(8,128)(2,1)}, u32[]{:S(2)}, u32[]{:S(2)}) %collective-permute-start.7) | collective-permute-done | bytes 524320 | tf_op jit(solution)/shard_map/ppermute | solution.py:14
  177.0 7.8 %convolution_convert_fusion = bf16[3,1024,2048]{2,1,0:T(8,128)(2,1)} fusion(bf16[256,3,1024]{0,2,1:T(8,128)(2,1)S(1)} %copy.16, bf16[128,2048]{1,0:T(8,128)(2,1)} %collective-permute-done.7, bf16[128,2048]{1,0:T(8,128)(2,1)S(1)} %maximum_select_fusion.1, pred[]{:T(512)S(6)} %eq.14), kind=kOutput, calls=%fused_computation.5 | convolution fusion | flops 3232235520 | bytes 15204353 | tf_op jit(solution)/shard_map/dot_general | solution.py:79
  (13 shorter events, 0.3 us)
Async XLA Ops:
  7.2 1.5 copy-start
  7.2 75.8 %all-gather.2.cloned.1.call-start = ((), (), s32[]{:S(2)}) async-start(), calls=%async_computation.1 | async-start | bytes 1966080 | tf_op jit(solution)/shard_map/all_gather | solution.py:60
  9.5 5.0 %copy-start.1 = (bf16[64,2048]{1,0:T(8,128)(2,1)S(1)}, bf16[64,2048]{1,0:T(8,128)(2,1)}, u32[]{:S(2)}) copy-start(bf16[64,2048]{1,0:T(8,128)(2,1)} %param.15) | copy-start | bytes 786436
  9.6 5.6 %copy-start.2 = (bf16[64,2048]{1,0:T(8,128)(2,1)S(1)}, bf16[64,2048]{1,0:T(8,128)(2,1)}, u32[]{:S(2)}) copy-start(bf16[64,2048]{1,0:T(8,128)(2,1)} %param.17) | copy-start | bytes 786436
  9.6 6.3 %copy-start.3 = (bf16[64,2048]{1,0:T(8,128)(2,1)S(1)}, bf16[64,2048]{1,0:T(8,128)(2,1)}, u32[]{:S(2)}) copy-start(bf16[64,2048]{1,0:T(8,128)(2,1)} %param.16) | copy-start | bytes 786436
  9.8 7.1 %collective-permute-start = (bf16[32,2048]{1,0:T(8,128)(2,1)S(1)}, bf16[32,2048]{1,0:T(8,128)(2,1)S(1)}, u32[]{:S(2)}, u32[]{:S(2)}) collective-permute-start(bf16[32,2048]{1,0:T(8,128)(2,1)S(1)} %get-tuple-element.31), channel_id=1, source_target_pairs={{0,1},{1,0},{2,3},{3,2},{4,5},{5,4},{6,7},{7,6},{8,9},{9,8},{10,11... | collective-permute-start | bytes 393224 | tf_op jit(solution)/shard_map/ppermute | solution.py:25
  12.8 7.6 %collective-permute-start.2 = (bf16[32,2048]{1,0:T(8,128)(2,1)S(1)}, bf16[32,2048]{1,0:T(8,128)(2,1)S(1)}, u32[]{:S(2)}, u32[]{:S(2)}) collective-permute-start(bf16[32,2048]{1,0:T(8,128)(2,1)S(1)} %get-tuple-element.32), channel_id=1, source_target_pairs={{0,3},{1,2},{2,1},{3,0},{4,7},{5,6},{6,5},{7,4},{8,11},{9,10},{10,... | collective-permute-start | bytes 393224 | tf_op jit(solution)/shard_map/ppermute | solution.py:25
  14.3 7.5 %collective-permute-start.1 = (bf16[32,2048]{1,0:T(8,128)(2,1)S(1)}, bf16[32,2048]{1,0:T(8,128)(2,1)S(1)}, u32[]{:S(2)}, u32[]{:S(2)}) collective-permute-start(bf16[32,2048]{1,0:T(8,128)(2,1)S(1)} %get-tuple-element.33), channel_id=1, source_target_pairs={{0,2},{1,3},{2,0},{3,1},{4,6},{5,7},{6,4},{7,5},{8,10},{9,11},{10,... | collective-permute-start | bytes 393224 | tf_op jit(solution)/shard_map/ppermute | solution.py:25
  22.1 0.8 collective-permute-start.3
  22.7 1.5 collective-permute-start.4
  25.8 103.2 %reduce-scatter.2.cloned.1.call-start = ((), (), s32[]{:S(2)}) async-start(), calls=%async_computation.2 | async-start | bytes 2359296 | tf_op jit(solution)/shard_map/reduce_scatter | solution.py:64
  92.7 36.3 %copy-start.4 = (bf16[32,2048]{1,0:T(8,128)(2,1)S(1)}, bf16[32,2048]{1,0:T(8,128)(2,1)}, u32[]{:S(2)}) copy-start(bf16[32,2048]{1,0:T(8,128)(2,1)} %param.21) | copy-start | bytes 393220
  92.7 36.3 %copy-start.5 = (f32[2048]{0:T(1024)S(1)}, f32[2048]{0:T(1024)}, u32[]{:S(2)}) copy-start(f32[2048]{0:T(1024)} %param.20) | copy-start | bytes 24580
  141.6 1.3 collective-permute-start.5
  143.0 8.4 %collective-permute-start.6 = (bf16[64,2048]{1,0:T(8,128)(2,1)S(1)}, bf16[64,2048]{1,0:T(8,128)(2,1)S(1)}, u32[]{:S(2)}, u32[]{:S(2)}) collective-permute-start(bf16[64,2048]{1,0:T(8,128)(2,1)S(1)} %maximum_select_fusion.2), channel_id=1, source_target_pairs={{0,8},{4,12},{8,0},{12,4},{16,24},{20,28},{24,16},{28,20},{1,9},{5... | collective-permute-start | bytes 786440 | tf_op jit(solution)/shard_map/ppermute | solution.py:14
  151.6 25.4 %collective-permute-start.7 = (bf16[128,2048]{1,0:T(8,128)(2,1)S(1)}, bf16[128,2048]{1,0:T(8,128)(2,1)}, u32[]{:S(2)}, u32[]{:S(2)}) collective-permute-start(bf16[128,2048]{1,0:T(8,128)(2,1)S(1)} %maximum_select_fusion.1), channel_id=1, source_target_pairs={{0,16},{4,20},{8,24},{12,28},{16,0},{20,4},{24,8},{28,12},{1,17},{... | collective-permute-start | bytes 1572872 | tf_op jit(solution)/shard_map/ppermute | solution.py:14
Sparse Core Ops, SparseCore 0:
  25.9 56.9 all-gather.1
  92.9 36.0 reduce-scatter.1
